TPU v7x, 32 devices: a whole 2x2x4 slice. The times are simulated.
32 devices in a mesh: ctx: 8 (over z, y), seq: 4 (over x, core).
Axes of the slice: x: 2, y: 2, z: 4, core: 2. Of those that a mesh axis runs over, the one named last changes fastest.
Arguments:
- tokens: bfloat16 [16384, 1024], P(('ctx', 'seq')), may hold values from -60 to 60
- w_qkv: bfloat16 [1024, 3072], replicated, may hold values from -1 to 1
- w_out: bfloat16 [1024, 1024], replicated, may hold values from -0.1875 to 0.1875
- counts: int32 [256], replicated, may hold values from 1 to 64
- rand_seg: int32 [256, 3], replicated, may hold values from 0 to 7, all different within a row; in each aligned block of 8 rows (0 to 7, 8 to 15, ...) at most 4 rows name the same one
- rand_off: int32 [256, 3], replicated, may hold values from 0 to 7
Outputs:
- mixed: bfloat16 [16384, 1024], P(('ctx', 'seq'))
Inputs may be any that keep to these rules, and one draw needn't show every extreme that they name: `rand_seg`: each row names 3 different segments; among the 8 rows of one device no segment is named more than 4 times, a bound that some block reaches.
All inputs are finite; a program needn't handle non-finite values.
Results may differ from a plain program's by a relative error of at most 0.0045.
The roundings to bfloat16 on the way count: a program that leaves them out, or rounds other values in their place, can miss the bound.
Values may be sent and summed in bfloat16 or wider, within the bound.
No kernel may reach another device: no remote copies, remote signals or barrier semaphores. Data moves between devices by JAX's collectives and lax.ppermute only.
A program may use at most 192 MiB of HBM per device.

v0:
```python
import math
import jax
import jax.numpy as jnp
from jax import lax
from jax.sharding import PartitionSpec as P

HD = 64
BLK = 64
RAND = 3
G_DEV = 8


def with_halo(block, sides, width):
    for axis, dim in sides:
        count = lax.axis_size(axis)
        forward = [(i, i + 1) for i in range(count - 1)]
        backward = [(target, source) for source, target in forward]
        low = lax.ppermute(
            lax.slice_in_dim(block, block.shape[dim] - width, None, axis=dim), axis, forward
        )
        high = lax.ppermute(lax.slice_in_dim(block, 0, width, axis=dim), axis, backward)
        block = jnp.concatenate([low, block, high], axis=dim)
    return block


def for_sending(x):

    def short(part):
        return part.astype(jnp.bfloat16) if part.dtype == jnp.float32 else part

    return jax.tree.map(short, x)


def attend(queries, nearby, distant, global_k, global_v, block_ids, far_ids, counts):
    span, block_len, head_count, head_dim = queries.shape
    width = head_count * head_dim
    block_total = counts.shape[0]
    scaling = 1.0 / math.sqrt(head_dim)
    key_parts = []
    value_parts = []
    part_counts = []
    for offset in range(3):
        piece = nearby[offset : offset + span]
        near_ids = block_ids + (offset - 1)
        existing = (near_ids >= 0) & (near_ids < block_total)
        part_counts.append(
            jnp.where(existing, jnp.take(counts, jnp.clip(near_ids, 0, block_total - 1)), 0)
        )
        key_parts.append(piece[..., :width].reshape(span, block_len, head_count, head_dim))
        value_parts.append(piece[..., width:].reshape(span, block_len, head_count, head_dim))
    for index in range(distant.shape[1]):
        piece = distant[:, index]
        part_counts.append(jnp.take(counts, far_ids[:, index]))
        key_parts.append(piece[..., :width].reshape(span, block_len, head_count, head_dim))
        value_parts.append(piece[..., width:].reshape(span, block_len, head_count, head_dim))
    positions = jnp.arange(block_len, dtype=jnp.int32)[None, None, None, :]
    score_parts = []
    for keys_now, count_now in zip(key_parts, part_counts):
        scores = (
            jnp.einsum("bqhd,bkhd->bhqk", queries, keys_now, preferred_element_type=jnp.float32)
            * scaling
        )
        score_parts.append(jnp.where(positions < count_now[:, None, None, None], scores, -jnp.inf))
    wide_scores = (
        jnp.einsum("bqhd,khd->bhqk", queries, global_k, preferred_element_type=jnp.float32)
        * scaling
    )
    peak_score = jnp.max(wide_scores, axis=-1)
    for scores in score_parts:
        peak_score = jnp.maximum(peak_score, jnp.max(scores, axis=-1))
    peak_score = peak_score[..., None]
    wide_exp = jnp.exp(wide_scores - peak_score)
    denominator = jnp.sum(wide_exp, axis=-1, keepdims=True)
    exp_parts = []
    for scores in score_parts:
        exps = jnp.exp(scores - peak_score)
        denominator = denominator + jnp.sum(exps, axis=-1, keepdims=True)
        exp_parts.append(exps)
    wide_prob = (wide_exp / denominator).astype(jnp.bfloat16)
    result = jnp.einsum("bhqk,khd->bqhd", wide_prob, global_v, preferred_element_type=jnp.float32)
    for exps, values_now in zip(exp_parts, value_parts):
        probs = (exps / denominator).astype(jnp.bfloat16)
        result = result + jnp.einsum(
            "bhqk,bkhd->bqhd", probs, values_now, preferred_element_type=jnp.float32
        )
    return result.astype(jnp.bfloat16)


def positions_among(owners, owner_count):
    marks = (owners[..., None] == jnp.arange(owner_count, dtype=jnp.int32)).astype(jnp.int32)
    ranks = jnp.cumsum(marks, axis=-2) - 1
    return jnp.sum(ranks * marks, axis=-1)


def serve_slots(owners, offsets, target, capacity):
    matched = owners == target
    ranks = jnp.cumsum(matched.astype(jnp.int32), axis=-1) - 1
    slot_hit = matched[..., None, :] & (
        ranks[..., None, :] == jnp.arange(capacity, dtype=jnp.int32)[:, None]
    )
    return jnp.sum(jnp.where(slot_hit, offsets[..., None, :], 0), axis=-1)


def run_groups(
    queries, near_blocks, distant, far_global, global_k, global_v, first_id, span, counts
):
    block_count = queries.shape[0]

    def one_group(start):
        group_queries = lax.dynamic_slice_in_dim(queries, start, span, 0)
        nearby = lax.dynamic_slice_in_dim(near_blocks, start, span + 2, 0)
        distant_part = lax.dynamic_slice_in_dim(distant, start, span, 0)
        far_ids = lax.dynamic_slice_in_dim(far_global, start, span, 0)
        block_ids = first_id + start + jnp.arange(span, dtype=jnp.int32)
        return attend(
            group_queries, nearby, distant_part, global_k, global_v, block_ids, far_ids, counts
        )

    starts = jnp.arange(block_count // span, dtype=jnp.int32) * span
    outputs = lax.map(one_group, starts)
    return outputs.reshape(block_count * queries.shape[1], -1)


def regroup(w_qkv, groups, head_total):
    model_dim = w_qkv.shape[0]
    shaped = w_qkv.reshape(model_dim, groups, head_total // groups, 3, HD)
    return jnp.transpose(shaped, (0, 1, 3, 2, 4)).reshape(model_dim, 3 * model_dim)


def local(tokens, w_qkv, w_out, counts, rand_seg, rand_off):
    seq_count = lax.axis_size("seq")
    ctx_count = lax.axis_size("ctx")
    seq_index = lax.axis_index("seq")
    ctx_index = lax.axis_index("ctx")
    tok_rows, model_dim = tokens.shape
    head_total = model_dim // HD
    head_local = head_total // seq_count
    seg_rows = tok_rows * seq_count
    seg_blocks = seg_rows // BLK
    dev_blocks = tok_rows // BLK
    local_width = head_local * HD
    capacity = (RAND * dev_blocks + ctx_count - 1) // ctx_count + 1
    first_block = (ctx_index * seq_count + seq_index) * dev_blocks
    own_counts = lax.dynamic_slice_in_dim(counts, first_block, dev_blocks)
    usable = (jnp.arange(BLK, dtype=jnp.int32)[None, :] < own_counts[:, None]).reshape(tok_rows)
    group_rows = tok_rows // G_DEV
    member = (
        jnp.arange(tok_rows, dtype=jnp.int32)[None, :] // group_rows
        == jnp.arange(G_DEV, dtype=jnp.int32)[:, None]
    )
    pooling = (member & usable[None, :]).astype(jnp.bfloat16)
    sums = jnp.dot(pooling, tokens, preferred_element_type=jnp.float32)
    pooled = sums / jnp.sum(pooling.astype(jnp.float32), axis=1, keepdims=True)
    summary = (pooled / jnp.sqrt(jnp.mean(pooled * pooled, axis=1, keepdims=True) + 1e-05)).astype(
        jnp.bfloat16
    )
    w_summary = w_qkv.reshape(model_dim, head_total, 3, HD)[:, :, 1:, :].reshape(
        model_dim, 2 * model_dim
    )
    summary_kv = jnp.dot(summary, w_summary, preferred_element_type=jnp.float32).astype(
        jnp.bfloat16
    )
    every_head = lax.all_gather(summary_kv, ("ctx", "seq"), axis=0, tiled=True)
    summary_heads = every_head.reshape(-1, head_total, 2, HD)
    all_owner = rand_seg.reshape(ctx_count, seq_count, dev_blocks * RAND)
    all_offset = rand_off.reshape(ctx_count, seq_count, dev_blocks * RAND)
    w_ordered = regroup(w_qkv, seq_count, head_total)
    qkv = jnp.dot(tokens, w_ordered, preferred_element_type=jnp.float32).astype(jnp.bfloat16)
    seg_qkv = lax.all_to_all(qkv, "seq", split_axis=1, concat_axis=0, tiled=True)
    my_heads = lax.dynamic_slice_in_dim(summary_heads, seq_index * head_local, head_local, 1)
    global_k = my_heads[:, :, 0, :]
    global_v = my_heads[:, :, 1, :]
    queries = seg_qkv[:, :local_width].reshape(seg_blocks, BLK, head_local, HD)
    own_kv = seg_qkv[:, local_width:]
    kv_cols = 2 * local_width
    rimmed = with_halo(own_kv, (("ctx", 0),), BLK)
    near_blocks = rimmed.reshape(seg_blocks + 2, BLK, kv_cols)
    seg_first = ctx_index * seg_blocks
    my_owner = lax.dynamic_slice_in_dim(rand_seg, seg_first, seg_blocks)
    my_offset = lax.dynamic_slice_in_dim(rand_off, seg_first, seg_blocks)
    block_rows = own_kv.reshape(seg_blocks, BLK * kv_cols)
    send_off = serve_slots(all_owner, all_offset, ctx_index, capacity)
    send_ids = send_off + (jnp.arange(seq_count, dtype=jnp.int32) * dev_blocks)[None, :, None]
    outgoing = jnp.take(block_rows, send_ids.reshape(-1), axis=0).reshape(
        ctx_count, seq_count * capacity, BLK * kv_cols
    )
    incoming = lax.all_to_all(outgoing, "ctx", split_axis=0, concat_axis=0, tiled=True)
    mine = my_owner.reshape(seq_count, dev_blocks * RAND)
    slot_ids = (
        mine * (seq_count * capacity)
        + jnp.arange(seq_count, dtype=jnp.int32)[:, None] * capacity
        + positions_among(mine, ctx_count)
    )
    fetched = jnp.take(
        incoming.reshape(ctx_count * seq_count * capacity, BLK * kv_cols),
        slot_ids.reshape(-1),
        axis=0,
    )
    distant = fetched.reshape(seg_blocks, RAND, BLK, kv_cols)
    slot_of_row = jnp.arange(seg_blocks, dtype=jnp.int32) // dev_blocks
    far_global = my_owner * seg_blocks + (slot_of_row * dev_blocks)[:, None] + my_offset
    attended = run_groups(
        queries, near_blocks, distant, far_global, global_k, global_v, seg_first, 8, counts
    )
    returned = lax.all_to_all(
        for_sending(attended), "seq", split_axis=0, concat_axis=1, tiled=True
    ).astype(attended.dtype)
    mixed = tokens.astype(jnp.float32) + jnp.dot(
        returned, w_out, preferred_element_type=jnp.float32
    )
    return mixed.astype(jnp.bfloat16)


def solution(mesh):
    in_specs = (P(("ctx", "seq"), None), P(), P(), P(), P(), P())
    out_specs = P(("ctx", "seq"), None)
    return jax.shard_map(local, mesh=mesh, in_specs=in_specs, out_specs=out_specs, check_vma=False)
```

profile of v0, /device:TPU:0, one launch (start us, length us, event | category | flops | bytes accessed | tf_op | source)
XLA Modules:
  0.0 729.9 jit_solution(17863630455531703478)
XLA Ops:
  6.5 8.8 %copy.355 = bf16[1024,3072]{0,1:T(8,128)(2,1)} copy(bf16[1024,3072]{1,0:T(8,128)(2,1)} %param.11) | data formatting | bytes 12582912 | tf_op args[1]
  15.4 3.6 copy.356
  19.0 3.7 convolution_convert_fusion
  24.6 4.8 all-to-all-start
  31.7 35.4 %all-to-all-done = bf16[512,4,768]{2,0,1:T(8,128)(2,1)} async-done(((bf16[512,4,768]{2,0,1:T(8,128)(2,1)}), bf16[512,4,768]{2,0,1:T(8,128)(2,1)}, u32[]{:S(2)}, u32[]{:S(2)}) %all-to-all-start) | async-done | bytes 3145760 | tf_op jit(solution)/shard_map/all_to_all | solution.py:169
  67.0 3.0 slice.118
  70.1 4.5 reshape.469
  74.5 31.8 %gather_fusion.6 = bf16[128,32768]{1,0:T(8,128)(2,1)} fusion(bf16[32,32768]{1,0:T(8,128)(2,1)} %reshape.469, s32[1024]{0:T(1024)S(1)} %pad_clamp_fusion.7), kind=kCustom, calls=%fused_computation.6 | custom fusion | bytes 16777728 | tf_op jit(solution)/shard_map/jit(_take)/gather | solution.py:184
  106.3 7.5 %broadcast_select_fusion = bf16[8,16,32768]{2,1,0:T(8,128)(2,1)} fusion(bf16[8,16,32768]{2,1,0:T(8,128)(2,1)} %bitcast.152, pred[8,16]{1,0:T(8,128)(4,1)S(1)} %compare_and_fusion), kind=kLoop, calls=%fused_computation.141 | loop fusion | flops 4194304 | bytes 16777344 | tf_op jit(solution)/shard_map/jit(_take)/select_n | solution.py:184
  113.8 6.6 all-to-all-start.1
  120.5 4.9 slice.116
  126.1 4.0 convolution_convert_fusion.1
  131.7 191.1 %all-gather.2.cloned.1.call-done = bf16[256,2048]{1,0:T(8,128)(2,1)} async-done(((bf16[8,2048]{1,0:T(8,128)(2,1)}), bf16[256,2048]{1,0:T(8,128)(2,1)}) %all-gather.2.cloned.1.call-update) | async-done | bytes 1048592 | tf_op jit(solution)/shard_map/all_gather | solution.py:163
  326.5 4.5 collective-permute-start
  334.9 3.1 pad_maximum_fusion
  338.0 17.1 %gather_fusion.7 = bf16[96,32768]{1,0:T(8,128)(2,1)} fusion(bf16[128,32768]{1,0:T(8,128)(2,1)} %bitcast.34, s32[1024]{0:T(1024)S(1)} %pad_clamp_fusion.6), kind=kCustom, calls=%fused_computation.7 | custom fusion | bytes 12583296 | tf_op jit(solution)/shard_map/jit(_take)/gather | solution.py:194
  355.1 5.3 copy.401
  360.4 3.3 copy_select_fusion
  363.7 335.4 %while.10 = (s32[]{:T(128)}, bf16[4,8,64,4,64]{2,1,4,3,0:T(8,128)(2,1)}, s32[4]{0:T(128)S(1)}, bf16[32,64,4,64]{3,2,1,0:T(4,128)(2,1)}, bf16[256,4,64]{0,2,1:T(8...) while((s32[]{:T(128)}, ...), condition=%wide.region_21.23_spmd, body=%wide.region_6.22_spmd.sunk | while | flops 347477696 | bytes 71337048 | solution.py:120
  371.9 2.7 constant_dynamic-slice_fusion.14
  391.9 3.2 fusion.128
  396.2 3.3 fusion.129
  402.4 3.2 fusion.131
  408.4 3.2 fusion.132
  417.0 3.3 fusion.134
  426.7 2.7 fusion.136
  434.6 2.5 fusion.138
  475.6 3.2 fusion.128
  480.0 3.3 fusion.129
  486.2 3.2 fusion.131
  492.2 3.2 fusion.132
  500.8 3.3 fusion.134
  510.5 2.7 fusion.136
  559.4 3.2 fusion.128
  563.7 3.3 fusion.129
  569.9 3.2 fusion.131
  575.9 3.2 fusion.132
  584.5 3.3 fusion.134
  594.3 2.7 fusion.136
  643.1 3.2 fusion.128
  647.5 3.3 fusion.129
  653.7 3.2 fusion.131
  659.7 3.2 fusion.132
  668.3 3.3 fusion.134
  678.0 2.7 fusion.136
  699.1 3.2 all_to_all.36
  702.3 16.9 %all_to_all.43 = bf16[4,512,256]{1,2,0:T(8,128)(2,1)S(1)} all-to-all(bf16[4,512,256]{1,2,0:T(8,128)(2,1)S(1)} %all_to_all.36), channel_id=1, replica_groups=mesh['ctx'=8,'seq'=4] {'seq'}, dimensions={0} | all-to-all | bytes 2097152 | tf_op jit(solution)/shard_map/all_to_all | solution.py:205
  719.2 3.5 add_convert_fusion
  (467 shorter events, 252.3 us)
Async XLA Ops:
  6.5 712.7 %copy-start = (bf16[1024,1024]{1,0:T(8,128)(2,1)S(1)}, bf16[1024,1024]{1,0:T(8,128)(2,1)}, u32[]{:S(2)}) copy-start(bf16[1024,1024]{1,0:T(8,128)(2,1)} %param.12) | copy-start | bytes 6291460
  15.4 3.6 copy-start.12
  24.6 4.8 copy-start.22
  24.6 5.1 copy-start.21
  24.6 42.5 %all-to-all-start = ((bf16[512,4,768]{2,0,1:T(8,128)(2,1)}), bf16[512,4,768]{2,0,1:T(8,128)(2,1)}, u32[]{:S(2)}, u32[]{:S(2)}) async-start(bf16[512,4,768]{2,0,1:T(8,128)(2,1)} %bitcast.156), calls=%async_computation | async-start | bytes 6291456 | tf_op jit(solution)/shard_map/all_to_all | solution.py:169
  30.7 43.8 %copy-start.23 = (s32[4]{0:T(128)}, s32[4]{0:T(128)S(1)}, u32[]{:S(2)}) copy-start(s32[4]{0:T(128)S(1)} %iota_multiply_fusion.1) | copy-start | bytes 52
  113.8 224.2 %all-to-all-start.1 = ((bf16[8,16,32768]{2,1,0:T(8,128)(2,1)}), bf16[8,16,32768]{2,1,0:T(8,128)(2,1)}, u32[]{:S(2)}, u32[]{:S(2)}) async-start(bf16[8,16,32768]{2,1,0:T(8,128)(2,1)} %broadcast_select_fusion), calls=%async_computation.1 | async-start | bytes 16777216 | tf_op jit(solution)/shard_map/all_to_all | solution.py:187
  120.4 202.5 %all-gather.2.cloned.1.call-start = ((), (), s32[]{:S(2)}) async-start(), calls=%async_computation.3 | async-start | bytes 1081344 | tf_op jit(solution)/shard_map/all_gather | solution.py:163
  120.4 5.0 copy-start.1
  325.2 9.7 %collective-permute-start.1 = (bf16[64,512]{1,0:T(8,128)(2,1)S(1)}, bf16[64,512]{1,0:T(8,128)(2,1)S(1)}, u32[]{:S(2)}, u32[]{:S(2)}) collective-permute-start(bf16[64,512]{1,0:T(8,128)(2,1)S(1)} %get-tuple-element.218), channel_id=1, source_target_pairs={{4,0},{8,4},{12,8},{16,12},{20,16},{24,20},{28,24},{5,1},{9,5},{13... | collective-permute-start | bytes 196616 | tf_op jit(solution)/shard_map/ppermute | solution.py:21
  326.5 8.4 %collective-permute-start = (bf16[64,512]{1,0:T(8,128)(2,1)S(1)}, bf16[64,512]{1,0:T(8,128)(2,1)S(1)}, u32[]{:S(2)}, u32[]{:S(2)}) collective-permute-start(bf16[64,512]{1,0:T(8,128)(2,1)S(1)} %get-tuple-element.217), channel_id=1, source_target_pairs={{0,4},{4,8},{8,12},{12,16},{16,20},{20,24},{24,28},{1,5},{5,9},{9,... | collective-permute-start | bytes 196616 | tf_op jit(solution)/shard_map/ppermute | solution.py:18
  360.4 3.3 copy-start.24
  396.1 3.4 copy-start.7
  396.1 6.2 copy-start.20
  400.2 7.4 %copy-start.19 = (s32[8]{0:T(128)S(1)}, s32[8]{0:T(128)}, u32[]{:S(2)}) copy-start(s32[8]{0:T(128)} %get-tuple-element.360) | copy-start | bytes 100 | tf_op jit(solution)/shard_map/while
  415.0 2.0 copy-start.3
  415.0 2.0 copy-start.4
  417.0 3.3 copy-start.2
  425.5 4.0 copy-start.9
  440.0 4.6 copy-start.10
  444.9 3.0 copy-start.25
  479.9 3.4 copy-start.7
  479.9 6.2 copy-start.20
  484.0 7.4 %copy-start.19 = (s32[8]{0:T(128)S(1)}, s32[8]{0:T(128)}, u32[]{:S(2)}) copy-start(s32[8]{0:T(128)} %get-tuple-element.360) | copy-start | bytes 100 | tf_op jit(solution)/shard_map/while
  498.8 2.0 copy-start.3
  498.8 2.0 copy-start.4
  500.8 3.3 copy-start.2
  509.2 4.0 copy-start.9
  523.8 4.6 copy-start.10
  528.7 3.0 copy-start.25
  563.6 3.4 copy-start.7
  563.6 6.2 copy-start.20
  567.8 7.4 %copy-start.19 = (s32[8]{0:T(128)S(1)}, s32[8]{0:T(128)}, u32[]{:S(2)}) copy-start(s32[8]{0:T(128)} %get-tuple-element.360) | copy-start | bytes 100 | tf_op jit(solution)/shard_map/while
  582.5 2.0 copy-start.3
  582.5 2.0 copy-start.4
  584.5 3.3 copy-start.2
  593.0 4.0 copy-start.9
  607.6 4.6 copy-start.10
  612.4 3.0 copy-start.25
  647.4 3.4 copy-start.7
  647.4 6.2 copy-start.20
  651.5 7.4 %copy-start.19 = (s32[8]{0:T(128)S(1)}, s32[8]{0:T(128)}, u32[]{:S(2)}) copy-start(s32[8]{0:T(128)} %get-tuple-element.360) | copy-start | bytes 100 | tf_op jit(solution)/shard_map/while
  666.3 2.0 copy-start.3
  666.3 2.0 copy-start.4
  668.3 3.3 copy-start.2
  676.8 4.0 copy-start.9
  691.3 4.6 copy-start.10
  696.2 2.9 copy-start.25
  (40 other events, 67.5 us)
Sparse Core Ops, SparseCore 0:
  130.3 192.5 all-gather.1
where the time goes:
time: 737 us; the launch traced here: 730 us
  local copies, waits for them, and re-layouts  229 us (31%)
  waiting for transfers between devices  227 us (31%)
  matrix products  149 us (20%)
  other arithmetic  61.5 us (8%)
  starting transfers between devices  17.3 us (2%)
  blocking collectives  16.9 us (2%)
  loops' own time  16 us (2%)
  between operations  14.1 us (2%)
    all_gather x1, waiting for transfers between devices, local(): every_head = lax.all_gather(summary_kv, ('ctx', 'seq'), axis=0, tiled=True)  191 us
    dot_general x24, matrix products, attend(): jnp.einsum('bqhd,bkhd->bhqk', queries, keys_now, preferred_element_type=j...  67.6 us
    dot_general x24, matrix products, attend(): jnp.einsum('bhqk,bkhd->bqhd', probs, values_now, preferred_element_type=j...  53.1 us
    reshape x24, local copies, waits for them, and re-layouts, attend(): piece[..., :width].reshape(span, block_len, head_count, head_dim)  41.3 us
    all_to_all x1, waiting for transfers between devices, local(): lax.all_to_all(qkv, 'seq', split_axis=1, concat_axis=0, tiled=True)  35.4 us
    gather x1, local copies, waits for them, and re-layouts, local(): jnp.take(block_rows, send_ids.reshape(-1), axis=0)  31.8 us
    reshape x24, local copies, waits for them, and re-layouts, attend(): piece[..., width:].reshape(span, block_len, head_count, head_dim)  31.4 us
    gather x1, local copies, waits for them, and re-layouts, local(): jnp.take(incoming.reshape(ctx_count * seq_count * capacity, BLK * kv_cols...  17.1 us
  transfers between devices with their start and end apart: 5, of which 2 were waited for; matrix products, arithmetic and copies ran while one was open for 3% of the time, Pallas kernels for 0%

commit v1 on v0

--- a/solution.py
+++ b/solution.py
@@ -166,7 +166,9 @@
     all_offset = rand_off.reshape(ctx_count, seq_count, dev_blocks * RAND)
     w_ordered = regroup(w_qkv, seq_count, head_total)
     qkv = jnp.dot(tokens, w_ordered, preferred_element_type=jnp.float32).astype(jnp.bfloat16)
-    seg_qkv = lax.all_to_all(qkv, "seq", split_axis=1, concat_axis=0, tiled=True)
+    pieces = jnp.split(qkv, lax.axis_size("seq"), axis=1)
+    received = lax.all_to_all(jnp.stack(pieces), "seq", 0, 0)
+    seg_qkv = jnp.concatenate(received, axis=0)
     my_heads = lax.dynamic_slice_in_dim(summary_heads, seq_index * head_local, head_local, 1)
     global_k = my_heads[:, :, 0, :]
     global_v = my_heads[:, :, 1, :]

time: 737 us -> 744 us (level)
  no operation moved by 1% of the time
where the time goes in v1:
time: 744 us; the launch traced here: 736 us
  local copies, waits for them, and re-layouts  231 us (31%)
  waiting for transfers between devices  227 us (31%)
  matrix products  149 us (20%)
  other arithmetic  66.7 us (9%)
  starting transfers between devices  17.3 us (2%)
  blocking collectives  16.9 us (2%)
  loops' own time  15.7 us (2%)
  between operations  14.1 us (2%)
    all_gather x1, waiting for transfers between devices, local(): every_head = lax.all_gather(summary_kv, ('ctx', 'seq'), axis=0, tiled=True)  191 us
    dot_general x24, matrix products, attend(): jnp.einsum('bqhd,bkhd->bhqk', queries, keys_now, preferred_element_type=j...  67.4 us
    dot_general x24, matrix products, attend(): jnp.einsum('bhqk,bkhd->bqhd', probs, values_now, preferred_element_type=j...  53.3 us
    reshape x24, local copies, waits for them, and re-layouts, attend(): piece[..., :width].reshape(span, block_len, head_count, head_dim)  41.3 us
    all_to_all x1, waiting for transfers between devices, local(): received = lax.all_to_all(jnp.stack(pieces), 'seq', 0, 0)  35.4 us
    gather x1, local copies, waits for them, and re-layouts, local(): jnp.take(block_rows, send_ids.reshape(-1), axis=0)  31.8 us
    reshape x24, local copies, waits for them, and re-layouts, attend(): piece[..., width:].reshape(span, block_len, head_count, head_dim)  31.2 us
    slice x12, local copies, waits for them, and re-layouts, attend(): piece[..., width:].reshape(span, block_len, head_count, head_dim)  20.7 us
  transfers between devices with their start and end apart: 5, of which 2 were waited for; matrix products, arithmetic and copies ran while one was open for 3% of the time, Pallas kernels for 0%

profile of v1, /device:TPU:0, one launch (start us, length us, event | category | flops | bytes accessed | tf_op | source)
XLA Modules:
  0.0 736.3 jit_solution(13135037306395041357)
XLA Ops:
  6.5 8.8 %copy.350 = bf16[1024,3072]{0,1:T(8,128)(2,1)} copy(bf16[1024,3072]{1,0:T(8,128)(2,1)} %param.11) | data formatting | bytes 12582912 | tf_op args[1]
  15.4 3.6 copy.351
  19.0 3.7 convolution_convert_fusion
  24.8 4.8 all-to-all-start
  31.9 35.4 %all-to-all-done = bf16[4,512,768]{2,1,0:T(8,128)(2,1)} async-done(((bf16[4,512,768]{2,1,0:T(8,128)(2,1)}), bf16[4,512,768]{2,1,0:T(8,128)(2,1)}, u32[]{:S(2)}, u32[]{:S(2)}) %all-to-all-start) | async-done | bytes 3145760 | tf_op jit(solution)/shard_map/all_to_all | solution.py:170
  67.3 3.0 slice.118
  70.3 4.5 reshape.470
  74.8 31.8 %gather_fusion.6 = bf16[128,32768]{1,0:T(8,128)(2,1)} fusion(bf16[32,32768]{1,0:T(8,128)(2,1)} %reshape.470, s32[1024]{0:T(1024)S(1)} %pad_clamp_fusion.7), kind=kCustom, calls=%fused_computation.6 | custom fusion | bytes 16777728 | tf_op jit(solution)/shard_map/jit(_take)/gather | solution.py:186
  106.6 7.5 %broadcast_select_fusion = bf16[8,16,32768]{2,1,0:T(8,128)(2,1)} fusion(bf16[8,16,32768]{2,1,0:T(8,128)(2,1)} %bitcast.154, pred[8,16]{1,0:T(8,128)(4,1)S(1)} %compare_and_fusion), kind=kLoop, calls=%fused_computation.141 | loop fusion | flops 4194304 | bytes 16777344 | tf_op jit(solution)/shard_map/jit(_take)/select_n | solution.py:186
  114.0 6.6 all-to-all-start.1
  120.7 4.9 slice.116
  126.4 4.0 convolution_convert_fusion.1
  131.9 191.1 %all-gather.2.cloned.1.call-done = bf16[256,2048]{1,0:T(8,128)(2,1)} async-done(((bf16[8,2048]{1,0:T(8,128)(2,1)}), bf16[256,2048]{1,0:T(8,128)(2,1)}) %all-gather.2.cloned.1.call-update) | async-done | bytes 1048592 | tf_op jit(solution)/shard_map/all_gather | solution.py:163
  326.7 4.5 collective-permute-start
  335.1 3.1 pad_maximum_fusion.1
  338.3 17.1 %gather_fusion.7 = bf16[96,32768]{1,0:T(8,128)(2,1)} fusion(bf16[128,32768]{1,0:T(8,128)(2,1)} %bitcast.36, s32[1024]{0:T(1024)S(1)} %pad_clamp_fusion.6), kind=kCustom, calls=%fused_computation.7 | custom fusion | bytes 12583296 | tf_op jit(solution)/shard_map/jit(_take)/gather | solution.py:196
  355.3 5.3 copy.394
  360.6 3.3 copy_select_fusion
  363.9 341.6 %while.10 = (s32[]{:T(128)}, bf16[4,8,64,4,64]{2,1,4,3,0:T(8,128)(2,1)}, s32[4]{0:T(128)S(1)}, bf16[32,64,4,64]{3,2,1,0:T(4,128)(2,1)}, bf16[256,4,64]{0,2,1:T(8...) while((s32[]{:T(128)}, ...), condition=%wide.region_21.23_spmd, body=%wide.region_6.22_spmd.sunk | while | flops 347477696 | bytes 69043080 | solution.py:120
  372.1 2.7 constant_dynamic-slice_fusion.14
  392.1 3.2 fusion.128
  396.4 3.3 fusion.129
  403.6 3.2 fusion.131
  409.5 3.2 fusion.132
  418.8 3.3 fusion.134
  428.5 2.7 fusion.136
  443.9 2.5 fusion.140
  477.4 3.2 fusion.128
  481.7 3.3 fusion.129
  488.9 3.2 fusion.131
  494.9 3.2 fusion.132
  504.2 3.3 fusion.134
  513.9 2.7 fusion.136
  562.7 3.2 fusion.128
  567.0 3.3 fusion.129
  574.2 3.2 fusion.131
  580.2 3.2 fusion.132
  589.5 3.3 fusion.134
  599.2 2.7 fusion.136
  648.0 3.2 fusion.128
  652.3 3.3 fusion.129
  659.5 3.2 fusion.131
  665.5 3.2 fusion.132
  674.8 3.3 fusion.134
  684.5 2.7 fusion.136
  705.5 3.2 all_to_all.22
  708.7 16.9 %all_to_all.29 = bf16[4,512,256]{1,2,0:T(8,128)(2,1)S(1)} all-to-all(bf16[4,512,256]{1,2,0:T(8,128)(2,1)S(1)} %all_to_all.22), channel_id=1, replica_groups=mesh['ctx'=8,'seq'=4] {'seq'}, dimensions={0} | all-to-all | bytes 2097152 | tf_op jit(solution)/shard_map/all_to_all | solution.py:207
  725.6 3.5 add_convert_fusion
  (412 shorter events, 259.2 us)
Async XLA Ops:
  6.5 719.1 %copy-start = (bf16[1024,1024]{1,0:T(8,128)(2,1)S(1)}, bf16[1024,1024]{1,0:T(8,128)(2,1)}, u32[]{:S(2)}) copy-start(bf16[1024,1024]{1,0:T(8,128)(2,1)} %param.12) | copy-start | bytes 6291460
  15.4 3.6 copy-start.10
  24.8 4.8 copy-start.15
  24.8 5.1 copy-start.14
  24.8 42.5 %all-to-all-start = ((bf16[4,512,768]{2,1,0:T(8,128)(2,1)}), bf16[4,512,768]{2,1,0:T(8,128)(2,1)}, u32[]{:S(2)}, u32[]{:S(2)}) async-start(bf16[4,512,768]{2,1,0:T(8,128)(2,1)} %pad_maximum_fusion), calls=%async_computation | async-start | bytes 6291456 | tf_op jit(solution)/shard_map/all_to_all | solution.py:170
  31.0 43.8 %copy-start.16 = (s32[4]{0:T(128)}, s32[4]{0:T(128)S(1)}, u32[]{:S(2)}) copy-start(s32[4]{0:T(128)S(1)} %iota_multiply_fusion.1) | copy-start | bytes 52
  114.0 224.2 %all-to-all-start.1 = ((bf16[8,16,32768]{2,1,0:T(8,128)(2,1)}), bf16[8,16,32768]{2,1,0:T(8,128)(2,1)}, u32[]{:S(2)}, u32[]{:S(2)}) async-start(bf16[8,16,32768]{2,1,0:T(8,128)(2,1)} %broadcast_select_fusion), calls=%async_computation.1 | async-start | bytes 16777216 | tf_op jit(solution)/shard_map/all_to_all | solution.py:189
  120.6 202.5 %all-gather.2.cloned.1.call-start = ((), (), s32[]{:S(2)}) async-start(), calls=%async_computation.3 | async-start | bytes 1081344 | tf_op jit(solution)/shard_map/all_gather | solution.py:163
  120.7 5.0 copy-start.1
  325.4 9.7 %collective-permute-start.1 = (bf16[64,512]{1,0:T(8,128)(2,1)S(1)}, bf16[64,512]{1,0:T(8,128)(2,1)S(1)}, u32[]{:S(2)}, u32[]{:S(2)}) collective-permute-start(bf16[64,512]{1,0:T(8,128)(2,1)S(1)} %get-tuple-element.218), channel_id=1, source_target_pairs={{4,0},{8,4},{12,8},{16,12},{20,16},{24,20},{28,24},{5,1},{9,5},{13... | collective-permute-start | bytes 196616 | tf_op jit(solution)/shard_map/ppermute | solution.py:21
  326.7 8.4 %collective-permute-start = (bf16[64,512]{1,0:T(8,128)(2,1)S(1)}, bf16[64,512]{1,0:T(8,128)(2,1)S(1)}, u32[]{:S(2)}, u32[]{:S(2)}) collective-permute-start(bf16[64,512]{1,0:T(8,128)(2,1)S(1)} %get-tuple-element.217), channel_id=1, source_target_pairs={{0,4},{4,8},{8,12},{12,16},{16,20},{20,24},{24,28},{1,5},{5,9},{9,... | collective-permute-start | bytes 196616 | tf_op jit(solution)/shard_map/ppermute | solution.py:18
  360.6 3.3 copy-start.17
  392.1 11.4 %copy-start.13 = (s32[8]{0:T(128)S(1)}, s32[8]{0:T(128)}, u32[]{:S(2)}) copy-start(s32[8]{0:T(128)} %get-tuple-element.361) | copy-start | bytes 100 | tf_op jit(solution)/shard_map/while
  396.4 12.4 %copy-start.12 = (s32[8]{0:T(128)S(1)}, s32[8]{0:T(128)}, u32[]{:S(2)}) copy-start(s32[8]{0:T(128)} %get-tuple-element.364) | copy-start | bytes 100 | tf_op jit(solution)/shard_map/while
  416.1 2.7 copy-start.3
  416.1 2.7 copy-start.4
  418.8 3.4 copy-start.2
  418.8 4.1 copy-start.11
  427.2 4.0 copy-start.8
  439.9 6.5 copy-start.9
  446.4 3.2 copy-start.18
  477.4 11.4 %copy-start.13 = (s32[8]{0:T(128)S(1)}, s32[8]{0:T(128)}, u32[]{:S(2)}) copy-start(s32[8]{0:T(128)} %get-tuple-element.361) | copy-start | bytes 100 | tf_op jit(solution)/shard_map/while
  481.7 12.4 %copy-start.12 = (s32[8]{0:T(128)S(1)}, s32[8]{0:T(128)}, u32[]{:S(2)}) copy-start(s32[8]{0:T(128)} %get-tuple-element.364) | copy-start | bytes 100 | tf_op jit(solution)/shard_map/while
  501.4 2.7 copy-start.3
  501.5 2.7 copy-start.4
  504.2 3.4 copy-start.2
  504.2 4.1 copy-start.11
  512.6 4.0 copy-start.8
  525.3 6.5 copy-start.9
  531.8 3.2 copy-start.18
  562.7 11.4 %copy-start.13 = (s32[8]{0:T(128)S(1)}, s32[8]{0:T(128)}, u32[]{:S(2)}) copy-start(s32[8]{0:T(128)} %get-tuple-element.361) | copy-start | bytes 100 | tf_op jit(solution)/shard_map/while
  567.0 12.4 %copy-start.12 = (s32[8]{0:T(128)S(1)}, s32[8]{0:T(128)}, u32[]{:S(2)}) copy-start(s32[8]{0:T(128)} %get-tuple-element.364) | copy-start | bytes 100 | tf_op jit(solution)/shard_map/while
  586.7 2.7 copy-start.3
  586.7 2.7 copy-start.4
  589.5 3.4 copy-start.2
  589.5 4.1 copy-start.11
  597.9 4.0 copy-start.8
  610.6 6.5 copy-start.9
  617.1 3.2 copy-start.18
  648.0 11.4 %copy-start.13 = (s32[8]{0:T(128)S(1)}, s32[8]{0:T(128)}, u32[]{:S(2)}) copy-start(s32[8]{0:T(128)} %get-tuple-element.361) | copy-start | bytes 100 | tf_op jit(solution)/shard_map/while
  652.3 12.4 %copy-start.12 = (s32[8]{0:T(128)S(1)}, s32[8]{0:T(128)}, u32[]{:S(2)}) copy-start(s32[8]{0:T(128)} %get-tuple-element.364) | copy-start | bytes 100 | tf_op jit(solution)/shard_map/while
  672.0 2.7 copy-start.3
  672.0 2.7 copy-start.4
  674.8 3.4 copy-start.2
  674.8 4.1 copy-start.11
  683.2 4.0 copy-start.8
  695.9 6.5 copy-start.9
  702.4 3.2 copy-start.18
  (12 other events, 17.5 us)
Sparse Core Ops, SparseCore 0:
  130.5 192.5 all-gather.1
